TPU v7x, 128 devices: a whole 4x4x4 slice. The times are simulated.
128 devices in a mesh: section: 2 (over x_lo), tok: 8 (over x_hi, z), mdl: 8 (over y, core).
Axes of the slice: x: 4 (x_hi: 2, x_lo: 2; x = x_hi * 2 + x_lo), y: 4, z: 4, core: 2. Of those that a mesh axis runs over, the one named last changes fastest.
Arguments:
- layer_input: bfloat16 [2, 2048, 2048], P(None, 'tok'), may hold values from -6 to 6
- segment_ids: int32 [2, 2048], replicated, may hold values from 0 to 3, as said below
- route_ids: int32 [2, 2048, 6], P(None, ('tok', 'mdl')), may hold values from 0 to 63, all different within a row; in each aligned block of 32 rows (0 to 31, 32 to 63, ..., all dimensions but the last counted through in order) at most 4 rows name the same one
- route_weights: float32 [2, 2048, 6], P(None, ('tok', 'mdl')), may hold values from 0.1 to 0.5
- attn_gain: float32 [2048], replicated, may hold values from 0.5 to 1.5
- w_query: bfloat16 [2048, 3072], P(None, 'mdl'), may hold values from -6.629126 to 6.629126
- w_kv_down: bfloat16 [2048, 576], replicated, may hold values from -0.13258252 to 0.13258252
- latent_gain: float32 [512], replicated, may hold values from 0.5 to 1.5
- w_kv_up: bfloat16 [512, 4096], P(None, 'mdl'), may hold values from -0.25 to 0.25
- w_out: bfloat16 [2048, 2048], P('mdl'), may hold values from -0.125 to 0.125
- ffn_gain: float32 [2048], replicated, may hold values from 0.5 to 1.5
- w_shared_gate: bfloat16 [2048, 2048], P(None, 'mdl'), may hold values from -0.125 to 0.125
- w_shared_up: bfloat16 [2048, 2048], P(None, 'mdl'), may hold values from -0.125 to 0.125
- w_shared_down: bfloat16 [2048, 2048], P('mdl'), may hold values from -0.125 to 0.125
- w_expert_gate: bfloat16 [64, 2048, 768], P(('tok', 'mdl')), may hold values from -0.125 to 0.125
- w_expert_up: bfloat16 [64, 2048, 768], P(('tok', 'mdl')), may hold values from -0.125 to 0.125
- w_expert_down: bfloat16 [64, 768, 2048], P(('tok', 'mdl')), may hold values from -0.21875 to 0.21875
Outputs:
- layer_output: bfloat16 [2, 2048, 2048], P('section', ('tok', 'mdl'))
Inputs may be any that keep to these rules, and one draw needn't show every extreme that they name: `segment_ids`: segment numbers never fall along a pack; each segment has 1 to 1024 tokens and one has exactly 1024. `route_ids`: each token names 6 different experts. In each aligned block of 32 tokens of a pack (the tokens of one device), no expert is named by more than 4 tokens, a bound that some block reaches.
All inputs are finite; a program needn't handle non-finite values.
Results may differ from a plain program's by a relative error of at most 0.02.
Values may be sent and summed in bfloat16 or wider, within the bound.
No kernel may reach another device: no remote copies, remote signals or barrier semaphores. Data moves between devices by JAX's collectives and lax.ppermute only.
A program may use at most 128 MiB of HBM per device.

v0:
```python
import math
import jax
import jax.numpy as jnp
from jax import lax
from jax.sharding import PartitionSpec as P

NOPE = 128
ROPE = 64
VDIM = 128
LATENT = 512
SEGS = 4
EPS = 1e-06


def passed_along(value, axis, steps):
    count = lax.axis_size(axis)
    initial, last = (max(0, -steps), min(count, count - steps))
    return lax.ppermute(value, axis, [(source, source + steps) for source in range(initial, last)])


def rms_scale(values, gain_vec):
    values = values.astype(jnp.float32)
    return values * lax.rsqrt(jnp.mean(values * values, axis=-1, keepdims=True) + EPS) * gain_vec


def rotary(values, positions):
    half_width = values.shape[-1] // 2
    frequency = 10000.0 ** (-jnp.arange(half_width, dtype=jnp.float32) / half_width)
    angles = positions.astype(jnp.float32)[:, None] * frequency[None, :]
    if values.ndim == 3:
        angles = angles[:, None, :]
    cosine = jnp.cos(angles)
    sine_part = jnp.sin(angles)
    lead_half = values[..., :half_width]
    tail_half = values[..., half_width:]
    return jnp.concatenate(
        [lead_half * cosine - tail_half * sine_part, lead_half * sine_part + tail_half * cosine],
        axis=-1,
    )


def positions_of(segment_row, segment_count):
    labels = jnp.arange(segment_count, dtype=jnp.int32)
    starts = jnp.sum((segment_row[None, :] < labels[:, None]).astype(jnp.int32), axis=1)
    member = (segment_row[:, None] == labels[None, :]).astype(jnp.int32)
    return jnp.arange(segment_row.shape[0], dtype=jnp.int32) - jnp.sum(
        member * starts[None, :], axis=1
    )


def shards(
    layer_input,
    segment_ids,
    route_ids,
    route_weights,
    attn_gain,
    w_query,
    w_kv_down,
    latent_gain,
    w_kv_up,
    w_out,
    ffn_gain,
    w_shared_gate,
    w_shared_up,
    w_shared_down,
    w_expert_gate,
    w_expert_up,
    w_expert_down,
):
    n_mdl = lax.axis_size("mdl")
    n_wide = lax.axis_size(("tok", "mdl"))
    section_id = lax.axis_index("section")
    tok_rank = lax.axis_index("tok")
    mdl_rank = lax.axis_index("mdl")
    micro_count, tok_dev, model_width = layer_input.shape
    row_dev = tok_dev // n_mdl
    top_count = route_ids.shape[2]
    local_heads = w_out.shape[0] // VDIM
    qk_width = NOPE + ROPE
    score_scale = 1.0 / math.sqrt(qk_width)
    expert_dev = w_expert_gate.shape[0]
    expert_total = expert_dev * n_wide
    capacity = max(2, 3 * row_dev * top_count // (2 * expert_total))
    slot_total = expert_total * capacity
    slot_ids = jnp.arange(slot_total, dtype=jnp.int32)
    expert_labels = jnp.arange(expert_total, dtype=jnp.int32)
    segment_row = lax.dynamic_index_in_dim(segment_ids, section_id, 0, keepdims=False)
    rows_in = lax.dynamic_index_in_dim(layer_input, section_id, 0, keepdims=False)
    expert_ids = lax.dynamic_index_in_dim(route_ids, section_id, 0, keepdims=False).reshape(-1)
    weight_rows = lax.dynamic_index_in_dim(route_weights, section_id, 0, keepdims=False)
    positions = positions_of(segment_row, SEGS)
    query_start = tok_rank * tok_dev
    query_pos = lax.dynamic_slice_in_dim(positions, query_start, tok_dev)
    query_seg = lax.dynamic_slice_in_dim(segment_row, query_start, tok_dev)
    query_index = query_start + jnp.arange(tok_dev, dtype=jnp.int32)
    normed = rms_scale(rows_in, attn_gain).astype(jnp.bfloat16)
    queries = jnp.dot(normed, w_query, preferred_element_type=jnp.float32).reshape(
        tok_dev, local_heads, qk_width
    )
    queries = jnp.concatenate(
        [queries[..., :NOPE], rotary(queries[..., NOPE:], query_pos)], axis=-1
    ).astype(jnp.bfloat16)
    compressed = jnp.dot(normed, w_kv_down, preferred_element_type=jnp.float32)
    latent = rms_scale(compressed[:, :LATENT], latent_gain).astype(jnp.bfloat16)
    key_rope = rotary(compressed[:, LATENT:], query_pos).astype(jnp.bfloat16)
    kv_rows = lax.all_gather(
        jnp.concatenate([latent, key_rope], axis=-1), "tok", axis=0, tiled=True
    )
    key_count = kv_rows.shape[0]
    expanded = (
        jnp.dot(kv_rows[:, :LATENT], w_kv_up, preferred_element_type=jnp.float32)
        .astype(jnp.bfloat16)
        .reshape(key_count, local_heads, NOPE + VDIM)
    )
    rope_keys = kv_rows[:, LATENT:]
    scores = jnp.einsum(
        "qhd,khd->hqk",
        queries[..., :NOPE],
        expanded[..., :NOPE],
        preferred_element_type=jnp.float32,
    )
    scores = scores + jnp.einsum(
        "qhd,kd->hqk", queries[..., NOPE:], rope_keys, preferred_element_type=jnp.float32
    )
    scores = scores * score_scale
    key_index = jnp.arange(key_count, dtype=jnp.int32)
    allowed = (segment_row[None, :] == query_seg[:, None]) & (
        key_index[None, :] <= query_index[:, None]
    )
    allowed = allowed[None, :, :]
    masked = jnp.where(allowed, scores, -1e30)
    row_max = jnp.max(masked, axis=-1, keepdims=True)
    weights = jnp.where(allowed, jnp.exp(scores - row_max), 0.0)
    totals = jnp.sum(weights, axis=-1, keepdims=True)
    weighted = jnp.einsum(
        "hqk,khd->hqd",
        weights.astype(jnp.bfloat16),
        expanded[..., NOPE:],
        preferred_element_type=jnp.float32,
    )
    attended = (
        (weighted / totals)
        .astype(jnp.bfloat16)
        .transpose(1, 0, 2)
        .reshape(tok_dev, local_heads * VDIM)
    )
    mixed_heads = lax.psum(
        jnp.dot(attended, w_out, preferred_element_type=jnp.float32).astype(jnp.bfloat16), "mdl"
    ).astype(jnp.float32)
    residual = (rows_in.astype(jnp.float32) + mixed_heads).astype(jnp.bfloat16)
    normed_ffn_all = rms_scale(residual, ffn_gain).astype(jnp.bfloat16)
    own_residual = lax.dynamic_slice_in_dim(residual, mdl_rank * row_dev, row_dev)
    normed_ffn = lax.dynamic_slice_in_dim(normed_ffn_all, mdl_rank * row_dev, row_dev)
    gate_proj = jnp.dot(normed_ffn_all, w_shared_gate, preferred_element_type=jnp.float32)
    up_proj = jnp.dot(normed_ffn_all, w_shared_up, preferred_element_type=jnp.float32)
    shared_act = (jax.nn.silu(gate_proj) * up_proj).astype(jnp.bfloat16)
    shared_out = lax.psum_scatter(
        jnp.dot(shared_act, w_shared_down, preferred_element_type=jnp.float32).astype(jnp.bfloat16),
        "mdl",
        scatter_dimension=0,
        tiled=True,
    ).astype(jnp.float32)
    onehot = (expert_ids[:, None] == expert_labels[None, :]).astype(jnp.int32)
    earlier = jnp.cumsum(onehot, axis=0) - onehot
    slot_index = jnp.sum(earlier * onehot, axis=1)
    target = expert_ids * capacity + slot_index
    placing = (
        (slot_ids[:, None] == target[None, :])
        .astype(jnp.int32)
        .reshape(slot_total, row_dev, top_count)
    )
    placing = jnp.sum(placing, axis=2).astype(jnp.bfloat16)
    outgoing = (
        jnp.dot(placing, normed_ffn, preferred_element_type=jnp.float32)
        .astype(jnp.bfloat16)
        .reshape(expert_total, capacity, model_width)
    )
    buffer = lax.all_to_all(outgoing, ("tok", "mdl"), split_axis=0, concat_axis=0, tiled=True)
    item_count = buffer.shape[1]
    grouped = (
        buffer.reshape(n_wide, expert_dev, item_count, model_width)
        .transpose(1, 0, 2, 3)
        .reshape(expert_dev, n_wide * item_count, model_width)
    )
    e_gate = jnp.einsum("erd,edf->erf", grouped, w_expert_gate, preferred_element_type=jnp.float32)
    e_up = jnp.einsum("erd,edf->erf", grouped, w_expert_up, preferred_element_type=jnp.float32)
    expert_act = (jax.nn.silu(e_gate) * e_up).astype(jnp.bfloat16)
    produced = jnp.einsum(
        "erf,efd->erd", expert_act, w_expert_down, preferred_element_type=jnp.float32
    ).astype(jnp.bfloat16)
    processed = (
        produced.reshape(expert_dev, n_wide, item_count, model_width)
        .transpose(1, 0, 2, 3)
        .reshape(n_wide * expert_dev, item_count, model_width)
    )
    returned = lax.all_to_all(processed, ("tok", "mdl"), split_axis=0, concat_axis=0, tiled=True)
    matched = target.reshape(row_dev, top_count)[:, :, None] == slot_ids[None, None, :]
    combining = jnp.sum(jnp.where(matched, weight_rows[:, :, None], 0.0), axis=1)
    routed = jnp.dot(
        combining,
        returned.reshape(slot_total, model_width).astype(jnp.float32),
        precision=lax.Precision.HIGHEST,
    )
    finished = (own_residual.astype(jnp.float32) + shared_out + routed).astype(jnp.bfloat16)
    return finished[None]


def solution(mesh):
    in_specs = (
        P(None, "tok", None),
        P(),
        P(None, ("tok", "mdl"), None),
        P(None, ("tok", "mdl"), None),
        P(),
        P(None, "mdl"),
        P(),
        P(),
        P(None, "mdl"),
        P("mdl", None),
        P(),
        P(None, "mdl"),
        P(None, "mdl"),
        P("mdl", None),
        P(("tok", "mdl"), None, None),
        P(("tok", "mdl"), None, None),
        P(("tok", "mdl"), None, None),
    )
    out_specs = P("section", ("tok", "mdl"), None)
    return jax.shard_map(shards, mesh=mesh, in_specs=in_specs, out_specs=out_specs, check_vma=False)
```

profile of v0, /device:TPU:1, one launch (start us, length us, event | category | flops | bytes accessed | tf_op | source)
XLA Modules:
  0.0 237.3 jit_solution(6687160402400603476)
XLA Ops:
  6.5 0.0 copy-start
  6.6 0.9 constant_dynamic-slice_fusion.2
  7.4 0.1 convert_reduce_fusion.1
  7.6 0.1 select_reduce_fusion.2
  7.7 1.5 fusion.22
  9.2 0.0 copy-start.11
  9.2 2.9 %fusion.53 = f32[256,576]{0,1:T(8,128)S(1)} fusion(bf16[2048,576]{0,1:T(8,128)(2,1)} %param.23, f32[2048]{0:T(1024)} %param.21, f32[256]{0:T(256)S(1)} %add_rsqrt_fusion.2, bf16[2,256,2048]{2,1,0:T(8,128)(2,1)} %param.17, s32[]{:T(128)S(6)} %select_n.33), kind=kOutput, calls=%fused_computation.52 | convolution fusion | flops 606076928 | bytes 4006916 | tf_op jit(solution)/shard_map/dot_general | solution.py:103
  12.1 0.8 copy-done.4
  12.9 0.1 multiply_reduce_fusion
  13.0 0.1 fusion.89
  13.1 1.0 multiply_cosine_fusion
  14.1 0.0 copy-start.12
  14.1 1.2 multiply_convert_fusion
  15.3 0.0 copy-start.14
  15.3 0.7 pad_maximum_fusion
  16.0 0.0 all-gather.2.cloned.1.call-update
  16.1 0.0 all-reduce.3.cloned.1.call-start
  16.1 2.6 %copy.37 = bf16[2048,384]{0,1:T(8,128)(2,1)} copy(bf16[2048,384]{1,0:T(8,128)(2,1)} %param.22) | data formatting | bytes 3145728 | tf_op args[5]
  18.8 0.1 copy.42
  18.9 0.1 eq.88
  19.0 0.6 reduce-window.6
  19.6 0.2 slice_reduce_fusion
  19.8 0.8 dynamic_slice.33
  20.6 2.4 %fusion.51 = f32[256,2,192]{0,2,1:T(8,128)S(1)} fusion(bf16[2,192,2048]{2,1,0:T(8,128)(2,1)} %bitcast.95, f32[2048]{0:T(1024)S(1)} %copy-done.14, f32[256]{0:T(256)S(1)} %add_rsqrt_fusion.2, bf16[2,256,2048]{2,1,0:T(8,128)(2,1)} %param.17, s32[]{:T(128)S(6)} %select_n.33), kind=kOutput, calls=%fused_computation.51 | convolution fusion | flops 404750336 | bytes 3023876 | tf_op jit(solution)/shard_map/dot_general | solution.py:97
  23.0 0.7 copy-done.7
  23.8 1.5 fusion.32
  25.3 49.9 %all-gather.2.cloned.1.call-done = bf16[2048,576]{0,1:T(8,128)(2,1)} async-done(((bf16[256,576]{0,1:T(8,128)(2,1)}), bf16[2048,576]{0,1:T(8,128)(2,1)}) %all-gather.2.cloned.1.call-update) | async-done | bytes 2359312 | tf_op jit(solution)/shard_map/all_gather | solution.py:106
  75.3 3.0 %convolution_convert_fusion = bf16[2048,512]{0,1:T(8,128)(2,1)S(1)} fusion(bf16[512,512]{1,0:T(8,128)(2,1)} %param.25, bf16[2048,576]{0,1:T(8,128)(2,1)} %all-gather.2.cloned.1.call-done), kind=kOutput, calls=%fused_computation.12 | convolution fusion | flops 1074790400 | bytes 4718592 | tf_op jit(solution)/shard_map/dot_general | solution.py:111
  78.3 0.7 fusion.56
  79.1 0.6 copy-done.6
  79.6 1.8 fusion.1
  81.4 1.7 fusion.99
  83.1 0.2 copy-done.3
  83.3 5.4 %fusion.47 = bf16[256,2,128]{0,2,1:T(8,128)(2,1)S(1)} fusion(bf16[2048,2,256]{0,2,1:T(8,128)(2,1)} %bitcast.97, f32[256,2]{0,1:T(2,128)S(1)} %bitcast.104, f32[2,256,2048]{2,1,0:T(8,128)} %copy-done.3, pred[256,2048]{1,0:T(8,128)(4,1)} %fusion.32), kind=kOutput, calls=%fused_computation.49 | convolution fusion | flops 272763392 | bytes 10618880 | tf_op jit(solution)/shard_map/hqk,khd->hqd/dot_general | solution.py:135
  88.8 0.0 slice-start
  88.8 2.7 %convolution_convert_fusion.2 = bf16[256,2048]{1,0:T(8,128)(2,1)} fusion(bf16[256,256]{0,1:T(8,128)(2,1)S(1)} %bitcast.101, bf16[256,2048]{1,0:T(8,128)(2,1)} %param.26), kind=kOutput, calls=%fused_computation.21 | convolution fusion | flops 268959744 | bytes 2228224 | tf_op jit(solution)/shard_map/dot_general | solution.py:148
  91.5 0.0 all-reduce.3.cloned.1.call-update
  91.5 0.1 bitcast_bitcast_fusion
  91.7 0.1 reduce_sum.90
  91.8 0.1 copy.45
  91.8 0.1 convert_reduce_fusion
  92.0 59.0 %all-reduce.3.cloned.1.call-done = bf16[256,2048]{1,0:T(8,128)(2,1)} async-done(((bf16[256,2048]{1,0:T(8,128)(2,1)}), bf16[256,2048]{1,0:T(8,128)(2,1)}) %all-reduce.3.cloned.1.call-update) | async-done | bytes 1048592 | tf_op jit(solution)/shard_map/psum | solution.py:147
  150.9 2.0 fusion.19
  153.0 1.0 copy-done.2
  154.0 0.3 fusion.21
  154.3 1.0 copy-done.1
  155.3 1.5 convolution_convert_fusion.3
  156.7 2.3 reshape.251
  159.0 10.7 %all-to-all-start = ((bf16[64,4,2048]{2,1,0:T(4,128)(2,1)}), bf16[64,4,2048]{2,1,0:T(4,128)(2,1)}, u32[]{:S(2)}, u32[]{:S(2)}) async-start(bf16[64,4,2048]{2,1,0:T(4,128)(2,1)} %reshape.251), calls=%async_computation.1 | async-start | bytes 2097152 | tf_op jit(solution)/shard_map/all_to_all | solution.py:178
  169.7 0.0 reduce-scatter.2.cloned.1.call-start
  169.8 2.0 fusion.100
  171.8 4.2 %convolution_convert_fusion.1 = bf16[256,2048]{1,0:T(8,128)(2,1)} fusion(bf16[256,2048]{1,0:T(8,128)(2,1)} %param.30, bf16[256,2048]{1,0:T(8,128)(2,1)} %copy-done.1, bf16[2048,256]{1,0:T(8,128)(2,1)} %param.29, f32[256,256]{1,0:T(8,128)S(1)} %fusion.100), kind=kOutput, calls=%fused_computation.20 | convolution fusion | flops 537788416 | bytes 4456448 | tf_op jit(solution)/shard_map/dot_general | solution.py:158
  176.0 0.0 reduce-scatter.2.cloned.1.call-update
  176.0 12.2 %all-to-all-done = bf16[64,4,2048]{2,1,0:T(4,128)(2,1)} async-done(((bf16[64,4,2048]{2,1,0:T(4,128)(2,1)}), bf16[64,4,2048]{2,1,0:T(4,128)(2,1)}, u32[]{:S(2)}, u32[]{:S(2)}) %all-to-all-start) | async-done | bytes 1048608 | tf_op jit(solution)/shard_map/all_to_all | solution.py:178
  188.2 2.1 reshape.252
  190.3 4.1 %fusion.9 = f32[256,768]{1,0:T(8,128)} fusion(bf16[256,2048]{1,0:T(8,128)(2,1)} %reshape.252, bf16[1,2048,768]{2,1,0:T(8,128)(2,1)} %param.31), kind=kOutput, calls=%fused_computation.10 | convolution fusion | flops 805306368 | bytes 4980736 | tf_op jit(solution)/shard_map/erd,edf->erf/dot_general | solution.py:185
  194.4 0.0 copy-done
  194.4 5.5 %fusion.14 = bf16[256,2048]{1,0:T(8,128)(2,1)} fusion(bf16[1,768,2048]{2,1,0:T(8,128)(2,1)S(1)} %copy-done, bf16[256,2048]{1,0:T(8,128)(2,1)} %reshape.252, bf16[1,2048,768]{2,1,0:T(8,128)(2,1)} %param.32, f32[256,768]{1,0:T(8,128)} %fusion.9), kind=kOutput, calls=%fused_computation.22 | convolution fusion | flops 1612316672 | bytes 9175040 | tf_op jit(solution)/shard_map/erf,efd->erd/dot_general | solution.py:188
  200.0 2.3 reshape_transpose_reshape.4
  202.3 5.4 %all-to-all-start.1 = ((bf16[64,4,2048]{2,1,0:T(4,128)(2,1)}), bf16[64,4,2048]{2,1,0:T(4,128)(2,1)}, u32[]{:S(2)}, u32[]{:S(2)}) async-start(bf16[64,4,2048]{2,1,0:T(4,128)(2,1)} %reshape_transpose_reshape.4), calls=%async_computation.2 | async-start | bytes 2097152 | tf_op jit(solution)/shard_map/all_to_all | solution.py:196
  207.7 0.1 select_reduce_fusion.1
  207.8 18.3 %all-to-all-done.1 = bf16[64,4,2048]{2,1,0:T(4,128)(2,1)} async-done(((bf16[64,4,2048]{2,1,0:T(4,128)(2,1)}), bf16[64,4,2048]{2,1,0:T(4,128)(2,1)}, u32[]{:S(2)}, u32[]{:S(2)}) %all-to-all-start.1) | async-done | bytes 1048608 | tf_op jit(solution)/shard_map/all_to_all | solution.py:196
  226.1 2.1 reshape.256
  228.2 2.6 %fusion.18 = bf16[1,32,2048]{2,1,0:T(8,128)(2,1)} fusion(f32[32,256]{1,0:T(8,128)S(1)} %select_reduce_fusion.1, bf16[256,2048]{1,0:T(8,128)(2,1)} %reshape.256, bf16[32,2048]{1,0:T(8,128)(2,1)} %reduce-scatter.2.cloned.1.call-done, bf16[256,2048]{1,0:T(8,128)(2,1)} %copy-done.2, s32[]{:T(128)S(6)} %select_n.39), kind=kOutput, calls=%fused_computation.26 | convolution fusion | flops 201654272 | bytes 1474564 | tf_op jit(solution)/shard_map/dot_general | solution.py:199
  (36 shorter events, 0.2 us)
Async XLA Ops:
  6.5 187.9 %copy-start = (bf16[1,768,2048]{2,1,0:T(8,128)(2,1)S(1)}, bf16[1,768,2048]{2,1,0:T(8,128)(2,1)}, u32[]{:S(2)}) copy-start(bf16[1,768,2048]{2,1,0:T(8,128)(2,1)} %param.33) | copy-start | bytes 9437188
  6.5 68.7 %all-gather.2.cloned.1.call-start = ((), (), s32[]{:S(2)}) async-start(), calls=%async_computation.3 | async-start | bytes 2654208 | tf_op jit(solution)/shard_map/all_gather | solution.py:106
  9.2 4.9 %copy-start.11 = (f32[512]{0:T(512)S(1)}, f32[512]{0:T(512)}, u32[]{:S(2)}) copy-start(f32[512]{0:T(512)} %param.24) | copy-start | bytes 6148
  12.1 0.8 copy-start.4
  14.1 4.7 %copy-start.12 = (s32[2,32,6]{1,0,2:T(2,128)S(1)}, s32[2,32,6]{1,0,2:T(2,128)}, u32[]{:S(2)}) copy-start(s32[2,32,6]{1,0,2:T(2,128)} %param.19) | copy-start | bytes 4612
  15.3 5.3 %copy-start.14 = (f32[2048]{0:T(1024)S(1)}, f32[2048]{0:T(1024)}, u32[]{:S(2)}) copy-start(f32[2048]{0:T(1024)} %param.21) | copy-start | bytes 24580
  16.1 134.9 %all-reduce.3.cloned.1.call-start = ((), (), s32[]{:S(2)}) async-start(), calls=%async_computation.4 | async-start | bytes 2097152 | tf_op jit(solution)/shard_map/psum | solution.py:147
  19.8 5.5 %copy-start.10 = (s32[64,3]{0,1:T(4,128)}, s32[64,3]{0,1:T(4,128)S(1)}, u32[]{:S(2)}) copy-start(s32[64,3]{0,1:T(4,128)S(1)} %reduce-window.9) | copy-start | bytes 2308
  23.0 0.7 copy-start.7
  75.3 3.0 %copy-start.8 = (f32[256,2,192]{0,2,1:T(8,128)S(1)}, f32[256,2,192]{0,2,1:T(8,128)}, u32[]{:S(2)}) copy-start(f32[256,2,192]{0,2,1:T(8,128)} %copy-done.7) | copy-start | bytes 1179652
  78.3 1.3 copy-start.6
  79.6 1.8 copy-start.5
  81.4 1.9 copy-start.3
  88.8 2.8 %slice-start = ((s32[64,3]{0,1:T(4,128)}), s32[64,2]{0,1:T(2,128)S(1)}, s32[]{:S(2)}) async-start(s32[64,3]{0,1:T(4,128)} %copy-done.10), calls=%async_computation.6 | async-start | bytes 2048 | tf_op jit(solution)/shard_map/slice.1
  91.5 62.5 %copy-start.9 = (f32[2048]{0:T(1024)S(1)}, f32[2048]{0:T(1024)}, u32[]{:S(2)}) copy-start(f32[2048]{0:T(1024)} %param.27) | copy-start | bytes 24580
  153.0 1.0 copy-start.2
  154.3 1.0 copy-start.1
  159.0 29.2 %all-to-all-start = ((bf16[64,4,2048]{2,1,0:T(4,128)(2,1)}), bf16[64,4,2048]{2,1,0:T(4,128)(2,1)}, u32[]{:S(2)}, u32[]{:S(2)}) async-start(bf16[64,4,2048]{2,1,0:T(4,128)(2,1)} %reshape.251), calls=%async_computation.1 | async-start | bytes 2097152 | tf_op jit(solution)/shard_map/all_to_all | solution.py:178
  169.7 58.5 %reduce-scatter.2.cloned.1.call-start = ((), (), s32[]{:S(2)}) async-start(), calls=%async_computation.5 | async-start | bytes 1179648 | tf_op jit(solution)/shard_map/reduce_scatter | solution.py:157
  200.0 7.7 %copy-start.13 = (f32[2,32,6]{1,0,2:T(2,128)S(1)}, f32[2,32,6]{1,0,2:T(2,128)}, u32[]{:S(2)}) copy-start(f32[2,32,6]{1,0,2:T(2,128)} %param.20) | copy-start | bytes 4612
  202.3 23.8 %all-to-all-start.1 = ((bf16[64,4,2048]{2,1,0:T(4,128)(2,1)}), bf16[64,4,2048]{2,1,0:T(4,128)(2,1)}, u32[]{:S(2)}, u32[]{:S(2)}) async-start(bf16[64,4,2048]{2,1,0:T(4,128)(2,1)} %reshape_transpose_reshape.4), calls=%async_computation.2 | async-start | bytes 2097152 | tf_op jit(solution)/shard_map/all_to_all | solution.py:196
Sparse Core Ops, SparseCore 0:
  16.2 59.0 all-gather.1
  91.6 59.2 all-reduce.2
  176.1 30.7 reduce-scatter.1
where the time goes:
time: 238 us; the launch traced here: 237 us
  waiting for transfers between devices  139 us (58%)
  matrix products  38.8 us (16%)
  local copies, waits for them, and re-layouts  18 us (8%)
  starting transfers between devices  16.2 us (7%)
  between operations  13.4 us (6%)
  other arithmetic  11.5 us (5%)
    psum x1, waiting for transfers between devices, shards(): lax.psum(jnp.dot(attended, w_out, preferred_element_type=jnp.float32).ast...  59 us
    all_gather x1, waiting for transfers between devices, shards(): lax.all_gather(jnp.concatenate([latent, key_rope], axis=-1), 'tok', axis=...  49.9 us
    all_to_all x1, waiting for transfers between devices, shards(): lax.all_to_all(processed, ('tok', 'mdl'), split_axis=0, concat_axis=0, ti...  18.3 us
    all_to_all x1, waiting for transfers between devices, shards(): lax.all_to_all(outgoing, ('tok', 'mdl'), split_axis=0, concat_axis=0, til...  12.2 us
    all_to_all x1, starting transfers between devices, shards(): lax.all_to_all(outgoing, ('tok', 'mdl'), split_axis=0, concat_axis=0, til...  10.7 us
    unnamed x32, local copies, waits for them, and re-layouts  6.91 us
    dot_general x1, matrix products, shards(): jnp.einsum('erf,efd->erd', expert_act, w_expert_down, preferred_element_t...  5.54 us
    dot_general x1, matrix products, shards(): jnp.einsum('hqk,khd->hqd', weights.astype(jnp.bfloat16), expanded[..., NO...  5.43 us
  transfers between devices with their start and end apart: 5, of which 4 were waited for; matrix products, arithmetic and copies ran while one was open for 13% of the time, Pallas kernels for 0%

commit v1 on v0

--- a/solution.py
+++ b/solution.py
@@ -10,6 +10,16 @@
 LATENT = 512
 SEGS = 4
 EPS = 1e-06
+
+
+def do_quarters(array_here, axis_no):
+    shelf = []
+    for _ in range(lax.axis_size("tok")):
+        shelf.append(array_here)
+    step_out = jnp.concatenate(
+        lax.all_to_all(jnp.stack(shelf), axis_name="tok", split_axis=0, concat_axis=0), axis=axis_no
+    )
+    return step_out
 
 
 def passed_along(value, axis, steps):
@@ -103,9 +113,7 @@
     compressed = jnp.dot(normed, w_kv_down, preferred_element_type=jnp.float32)
     latent = rms_scale(compressed[:, :LATENT], latent_gain).astype(jnp.bfloat16)
     key_rope = rotary(compressed[:, LATENT:], query_pos).astype(jnp.bfloat16)
-    kv_rows = lax.all_gather(
-        jnp.concatenate([latent, key_rope], axis=-1), "tok", axis=0, tiled=True
-    )
+    kv_rows = do_quarters(jnp.concatenate([latent, key_rope], axis=-1), 0)
     key_count = kv_rows.shape[0]
     expanded = (
         jnp.dot(kv_rows[:, :LATENT], w_kv_up, preferred_element_type=jnp.float32)

time: 238 us -> 219 us (0.920)
  waiting for transfers between devices: 139 us -> 111 us
  starting transfers between devices: 16.2 us -> 24.7 us
  local copies, waits for them, and re-layouts: 18 us -> 21.8 us
  matrix products: 38.8 us -> 36.1 us
    all_gather x1 -> x0, waiting for transfers between devices: 49.9 us -> none  [shards(): lax.all_gather(jnp.concatenate([latent, key_rope], axis=-1), 'tok', axis=...]
    all_to_all x0 -> x1, waiting for transfers between devices: none -> 19.8 us  [do_quarters(): lax.all_to_all(jnp.stack(shelf), axis_name='tok', split_axis=0, concat_ax...]
    all_to_all x0 -> x1, starting transfers between devices: none -> 8.31 us  [do_quarters(): lax.all_to_all(jnp.stack(shelf), axis_name='tok', split_axis=0, concat_ax...]
    unnamed x32 -> x34, local copies, waits for them, and re-layouts: 6.91 us -> 7.19 us
  transfers between devices with their start and end apart: 5 -> 5, of which waited for: 4 -> 4; matrix products, arithmetic and copies ran while one was open for 13% -> 14% of each run, Pallas kernels for 0% -> 0%
where the time goes in v1:
time: 219 us; the launch traced here: 218 us
  waiting for transfers between devices  111 us (51%)
  matrix products  36.1 us (16%)
  starting transfers between devices  24.7 us (11%)
  local copies, waits for them, and re-layouts  21.8 us (10%)
  between operations  13.7 us (6%)
  other arithmetic  10.8 us (5%)
    psum x1, waiting for transfers between devices, shards(): lax.psum(jnp.dot(attended, w_out, preferred_element_type=jnp.float32).ast...  60.2 us
    all_to_all x1, waiting for transfers between devices, do_quarters(): lax.all_to_all(jnp.stack(shelf), axis_name='tok', split_axis=0, concat_ax...  19.8 us
    all_to_all x1, waiting for transfers between devices, shards(): lax.all_to_all(processed, ('tok', 'mdl'), split_axis=0, concat_axis=0, ti...  18.3 us
    all_to_all x1, waiting for transfers between devices, shards(): lax.all_to_all(outgoing, ('tok', 'mdl'), split_axis=0, concat_axis=0, til...  12.2 us
    all_to_all x1, starting transfers between devices, shards(): lax.all_to_all(outgoing, ('tok', 'mdl'), split_axis=0, concat_axis=0, til...  10.9 us
    all_to_all x1, starting transfers between devices, do_quarters(): lax.all_to_all(jnp.stack(shelf), axis_name='tok', split_axis=0, concat_ax...  8.31 us
    unnamed x34, local copies, waits for them, and re-layouts  7.19 us
    dot_general x1, matrix products, shards(): jnp.einsum('erf,efd->erd', expert_act, w_expert_down, preferred_element_t...  5.53 us
  transfers between devices with their start and end apart: 5, of which 4 were waited for; matrix products, arithmetic and copies ran while one was open for 14% of the time, Pallas kernels for 0%

profile of v1, /device:TPU:1, one launch (start us, length us, event | category | flops | bytes accessed | tf_op | source)
XLA Modules:
  0.0 217.7 jit_solution(15773290859829670427)
XLA Ops:
  6.5 0.0 copy-start
  6.6 0.9 constant_dynamic-slice_fusion.2
  7.4 0.1 convert_reduce_fusion.1
  7.6 0.1 select_reduce_fusion.2
  7.7 1.5 fusion.22
  9.2 0.0 copy-start.11
  9.2 2.9 %fusion.53 = f32[256,576]{0,1:T(8,128)S(1)} fusion(bf16[2048,576]{0,1:T(8,128)(2,1)} %param.23, f32[2048]{0:T(1024)} %param.21, f32[256]{0:T(256)S(1)} %add_rsqrt_fusion.2, bf16[2,256,2048]{2,1,0:T(8,128)(2,1)} %param.17, s32[]{:T(128)S(6)} %select_n.33), kind=kOutput, calls=%fused_computation.52 | convolution fusion | flops 606076928 | bytes 4006916 | tf_op jit(solution)/shard_map/dot_general | solution.py:113
  12.1 0.8 copy-done.4
  12.9 0.1 multiply_reduce_fusion
  13.0 0.1 fusion.89
  13.1 1.0 multiply_cosine_fusion
  14.1 1.2 multiply_convert_fusion
  15.3 1.5 stack.2
  16.8 8.3 %all-to-all-start = ((bf16[8,256,576]{1,2,0:T(8,128)(2,1)}), bf16[8,256,576]{1,2,0:T(8,128)(2,1)}, u32[]{:S(2)}, u32[]{:S(2)}) async-start(bf16[8,256,576]{1,2,0:T(8,128)(2,1)} %stack.2), calls=%async_computation | async-start | bytes 4718592 | tf_op jit(solution)/shard_map/all_to_all | solution.py:20
  25.2 0.0 copy-start.15
  25.2 0.0 all-reduce.3.cloned.1.call-start
  25.2 2.6 %copy.51 = bf16[2048,384]{0,1:T(8,128)(2,1)} copy(bf16[2048,384]{1,0:T(8,128)(2,1)} %param.22) | data formatting | bytes 3145728 | tf_op args[5]
  27.9 0.1 copy.57
  28.0 0.1 eq.88
  28.1 0.6 reduce-window.6
  28.7 0.2 slice_reduce_fusion
  28.9 0.8 dynamic_slice.33
  29.7 2.4 %fusion.51 = f32[256,2,192]{0,2,1:T(8,128)S(1)} fusion(bf16[2,192,2048]{2,1,0:T(8,128)(2,1)} %bitcast.99, f32[2048]{0:T(1024)S(1)} %copy-done.15, f32[256]{0:T(256)S(1)} %add_rsqrt_fusion.2, bf16[2,256,2048]{2,1,0:T(8,128)(2,1)} %param.17, s32[]{:T(128)S(6)} %select_n.33), kind=kOutput, calls=%fused_computation.51 | convolution fusion | flops 404750336 | bytes 3023876 | tf_op jit(solution)/shard_map/dot_general | solution.py:107
  32.1 0.7 copy-done.7
  32.9 1.5 fusion.32
  34.4 19.8 %all-to-all-done = bf16[8,256,576]{1,2,0:T(8,128)(2,1)} async-done(((bf16[8,256,576]{1,2,0:T(8,128)(2,1)}), bf16[8,256,576]{1,2,0:T(8,128)(2,1)}, u32[]{:S(2)}, u32[]{:S(2)}) %all-to-all-start) | async-done | bytes 2359328 | tf_op jit(solution)/shard_map/all_to_all | solution.py:20
  54.3 2.0 copy.69
  56.3 1.3 convolution_convert_fusion
  57.7 0.7 fusion.56
  58.4 0.6 copy-done.6
  59.0 0.8 fusion.1
  59.8 0.3 copy-done.5
  60.0 1.7 fusion.99
  61.8 0.2 copy-done.3
  62.0 5.4 %fusion.47 = bf16[256,2,128]{0,2,1:T(8,128)(2,1)S(1)} fusion(bf16[2048,2,256]{0,2,1:T(8,128)(2,1)} %bitcast.101, f32[256,2]{0,1:T(2,128)S(1)} %bitcast.108, f32[2,256,2048]{2,1,0:T(8,128)} %copy-done.3, pred[256,2048]{1,0:T(8,128)(4,1)} %fusion.32), kind=kOutput, calls=%fused_computation.49 | convolution fusion | flops 272763392 | bytes 10618880 | tf_op jit(solution)/shard_map/hqk,khd->hqd/dot_general | solution.py:143
  67.4 0.0 slice-start
  67.4 2.7 %convolution_convert_fusion.2 = bf16[256,2048]{1,0:T(8,128)(2,1)} fusion(bf16[256,256]{0,1:T(8,128)(2,1)S(1)} %bitcast.105, bf16[256,2048]{1,0:T(8,128)(2,1)} %param.26), kind=kOutput, calls=%fused_computation.21 | convolution fusion | flops 268959744 | bytes 2228224 | tf_op jit(solution)/shard_map/dot_general | solution.py:156
  70.1 0.0 all-reduce.3.cloned.1.call-update
  70.2 0.1 bitcast_bitcast_fusion
  70.3 0.1 reduce_sum.90
  70.4 0.1 copy.60
  70.5 0.1 convert_reduce_fusion
  70.6 60.2 %all-reduce.3.cloned.1.call-done = bf16[256,2048]{1,0:T(8,128)(2,1)} async-done(((bf16[256,2048]{1,0:T(8,128)(2,1)}), bf16[256,2048]{1,0:T(8,128)(2,1)}) %all-reduce.3.cloned.1.call-update) | async-done | bytes 1048592 | tf_op jit(solution)/shard_map/psum | solution.py:155
  130.8 2.0 fusion.19
  132.9 1.0 copy-done.2
  133.9 0.3 fusion.21
  134.2 1.0 copy-done.1
  135.2 1.5 convolution_convert_fusion.3
  136.7 2.3 %reshape.257 = bf16[64,4,2048]{2,1,0:T(4,128)(2,1)} reshape(bf16[256,2048]{1,0:T(8,128)(2,1)} %convolution_convert_fusion.3) | data formatting | bytes 2097152 | tf_op jit(solution)/shard_map/reshape | solution.py:184
  138.9 10.9 %all-to-all-start.1 = ((bf16[64,4,2048]{2,1,0:T(4,128)(2,1)}), bf16[64,4,2048]{2,1,0:T(4,128)(2,1)}, u32[]{:S(2)}, u32[]{:S(2)}) async-start(bf16[64,4,2048]{2,1,0:T(4,128)(2,1)} %reshape.257), calls=%async_computation.2 | async-start | bytes 2097152 | tf_op jit(solution)/shard_map/all_to_all | solution.py:186
  149.8 0.0 reduce-scatter.2.cloned.1.call-start
  149.9 2.0 fusion.100
  151.9 4.2 %convolution_convert_fusion.1 = bf16[256,2048]{1,0:T(8,128)(2,1)} fusion(bf16[256,2048]{1,0:T(8,128)(2,1)} %param.30, bf16[256,2048]{1,0:T(8,128)(2,1)} %copy-done.1, bf16[2048,256]{1,0:T(8,128)(2,1)} %param.29, f32[256,256]{1,0:T(8,128)S(1)} %fusion.100), kind=kOutput, calls=%fused_computation.20 | convolution fusion | flops 537788416 | bytes 4456448 | tf_op jit(solution)/shard_map/dot_general | solution.py:166
  156.1 0.0 reduce-scatter.2.cloned.1.call-update
  156.1 12.2 %all-to-all-done.1 = bf16[64,4,2048]{2,1,0:T(4,128)(2,1)} async-done(((bf16[64,4,2048]{2,1,0:T(4,128)(2,1)}), bf16[64,4,2048]{2,1,0:T(4,128)(2,1)}, u32[]{:S(2)}, u32[]{:S(2)}) %all-to-all-start.1) | async-done | bytes 1048608 | tf_op jit(solution)/shard_map/all_to_all | solution.py:186
  168.3 2.1 reshape.258
  170.4 4.1 %fusion.9 = f32[256,768]{1,0:T(8,128)} fusion(bf16[256,2048]{1,0:T(8,128)(2,1)} %reshape.258, bf16[1,2048,768]{2,1,0:T(8,128)(2,1)} %param.31), kind=kOutput, calls=%fused_computation.10 | convolution fusion | flops 805306368 | bytes 4980736 | tf_op jit(solution)/shard_map/erd,edf->erf/dot_general | solution.py:193
  174.5 5.5 %fusion.14 = bf16[256,2048]{1,0:T(8,128)(2,1)} fusion(bf16[1,768,2048]{2,1,0:T(8,128)(2,1)S(1)} %copy-done, bf16[256,2048]{1,0:T(8,128)(2,1)} %reshape.258, bf16[1,2048,768]{2,1,0:T(8,128)(2,1)} %param.32, f32[256,768]{1,0:T(8,128)} %fusion.9), kind=kOutput, calls=%fused_computation.22 | convolution fusion | flops 1612316672 | bytes 9175040 | tf_op jit(solution)/shard_map/erf,efd->erd/dot_general | solution.py:196
  180.1 2.3 %reshape_transpose_reshape.4 = bf16[64,4,2048]{2,1,0:T(4,128)(2,1)} reshape(bf16[256,2048]{1,0:T(8,128)(2,1)} %fusion.14) | data formatting | bytes 2097152 | tf_op jit(solution)/shard_map/reshape;transpose;reshape | solution.py:202
  182.4 5.4 %all-to-all-start.2 = ((bf16[64,4,2048]{2,1,0:T(4,128)(2,1)}), bf16[64,4,2048]{2,1,0:T(4,128)(2,1)}, u32[]{:S(2)}, u32[]{:S(2)}) async-start(bf16[64,4,2048]{2,1,0:T(4,128)(2,1)} %reshape_transpose_reshape.4), calls=%async_computation.3 | async-start | bytes 2097152 | tf_op jit(solution)/shard_map/all_to_all | solution.py:204
  187.8 0.1 select_reduce_fusion.1
  187.9 18.3 %all-to-all-done.2 = bf16[64,4,2048]{2,1,0:T(4,128)(2,1)} async-done(((bf16[64,4,2048]{2,1,0:T(4,128)(2,1)}), bf16[64,4,2048]{2,1,0:T(4,128)(2,1)}, u32[]{:S(2)}, u32[]{:S(2)}) %all-to-all-start.2) | async-done | bytes 1048608 | tf_op jit(solution)/shard_map/all_to_all | solution.py:204
  206.2 2.1 reshape.262
  208.3 2.6 %fusion.18 = bf16[1,32,2048]{2,1,0:T(8,128)(2,1)} fusion(f32[32,256]{1,0:T(8,128)S(1)} %select_reduce_fusion.1, bf16[256,2048]{1,0:T(8,128)(2,1)} %reshape.262, bf16[32,2048]{1,0:T(8,128)(2,1)} %reduce-scatter.2.cloned.1.call-done, bf16[256,2048]{1,0:T(8,128)(2,1)} %copy-done.2, s32[]{:T(128)S(6)} %select_n.39), kind=kOutput, calls=%fused_computation.26 | convolution fusion | flops 201654272 | bytes 1474564 | tf_op jit(solution)/shard_map/dot_general | solution.py:207
  (39 shorter events, 0.2 us)
Async XLA Ops:
  6.5 168.0 %copy-start = (bf16[1,768,2048]{2,1,0:T(8,128)(2,1)S(1)}, bf16[1,768,2048]{2,1,0:T(8,128)(2,1)}, u32[]{:S(2)}) copy-start(bf16[1,768,2048]{2,1,0:T(8,128)(2,1)} %param.33) | copy-start | bytes 9437188
  9.2 4.9 %copy-start.11 = (f32[512]{0:T(512)S(1)}, f32[512]{0:T(512)}, u32[]{:S(2)}) copy-start(f32[512]{0:T(512)} %param.24) | copy-start | bytes 6148
  12.1 0.8 copy-start.4
  16.8 37.4 %all-to-all-start = ((bf16[8,256,576]{1,2,0:T(8,128)(2,1)}), bf16[8,256,576]{1,2,0:T(8,128)(2,1)}, u32[]{:S(2)}, u32[]{:S(2)}) async-start(bf16[8,256,576]{1,2,0:T(8,128)(2,1)} %stack.2), calls=%async_computation | async-start | bytes 4718592 | tf_op jit(solution)/shard_map/all_to_all | solution.py:20
  25.2 2.7 %copy-start.12 = (s32[2,32,6]{1,0,2:T(2,128)S(1)}, s32[2,32,6]{1,0,2:T(2,128)}, u32[]{:S(2)}) copy-start(s32[2,32,6]{1,0,2:T(2,128)} %param.19) | copy-start | bytes 4612
  25.2 4.5 %copy-start.15 = (f32[2048]{0:T(1024)S(1)}, f32[2048]{0:T(1024)}, u32[]{:S(2)}) copy-start(f32[2048]{0:T(1024)} %param.21) | copy-start | bytes 24580
  25.2 105.7 %all-reduce.3.cloned.1.call-start = ((), (), s32[]{:S(2)}) async-start(), calls=%async_computation.4 | async-start | bytes 2097152 | tf_op jit(solution)/shard_map/psum | solution.py:155
  28.9 5.5 %copy-start.10 = (s32[64,3]{0,1:T(4,128)}, s32[64,3]{0,1:T(4,128)S(1)}, u32[]{:S(2)}) copy-start(s32[64,3]{0,1:T(4,128)S(1)} %reduce-window.9) | copy-start | bytes 2308
  32.1 0.8 copy-start.7
  54.3 2.0 copy-start.14
  56.3 1.4 copy-start.8
  57.7 1.3 copy-start.6
  59.0 1.0 copy-start.5
  60.0 1.9 copy-start.3
  67.4 2.8 %slice-start = ((s32[64,3]{0,1:T(4,128)}), s32[64,2]{0,1:T(2,128)S(1)}, s32[]{:S(2)}) async-start(s32[64,3]{0,1:T(4,128)} %copy-done.10), calls=%async_computation.6 | async-start | bytes 2048 | tf_op jit(solution)/shard_map/slice.1
  70.1 63.8 %copy-start.9 = (f32[2048]{0:T(1024)S(1)}, f32[2048]{0:T(1024)}, u32[]{:S(2)}) copy-start(f32[2048]{0:T(1024)} %param.27) | copy-start | bytes 24580
  132.9 1.0 copy-start.2
  134.2 1.0 copy-start.1
  138.9 29.4 %all-to-all-start.1 = ((bf16[64,4,2048]{2,1,0:T(4,128)(2,1)}), bf16[64,4,2048]{2,1,0:T(4,128)(2,1)}, u32[]{:S(2)}, u32[]{:S(2)}) async-start(bf16[64,4,2048]{2,1,0:T(4,128)(2,1)} %reshape.257), calls=%async_computation.2 | async-start | bytes 2097152 | tf_op jit(solution)/shard_map/all_to_all | solution.py:186
  149.8 58.5 %reduce-scatter.2.cloned.1.call-start = ((), (), s32[]{:S(2)}) async-start(), calls=%async_computation.5 | async-start | bytes 1179648 | tf_op jit(solution)/shard_map/reduce_scatter | solution.py:165
  180.1 7.7 %copy-start.13 = (f32[2,32,6]{1,0,2:T(2,128)S(1)}, f32[2,32,6]{1,0,2:T(2,128)}, u32[]{:S(2)}) copy-start(f32[2,32,6]{1,0,2:T(2,128)} %param.20) | copy-start | bytes 4612
  182.4 23.8 %all-to-all-start.2 = ((bf16[64,4,2048]{2,1,0:T(4,128)(2,1)}), bf16[64,4,2048]{2,1,0:T(4,128)(2,1)}, u32[]{:S(2)}, u32[]{:S(2)}) async-start(bf16[64,4,2048]{2,1,0:T(4,128)(2,1)} %reshape_transpose_reshape.4), calls=%async_computation.3 | async-start | bytes 2097152 | tf_op jit(solution)/shard_map/all_to_all | solution.py:204
Sparse Core Ops, SparseCore 0:
  70.3 60.5 all-reduce.2
  156.2 30.7 reduce-scatter.1
